TPU v7x, 256 devices: a whole 4x4x8 slice. The times are simulated.
256 devices in a mesh: member: 8 (over x, y_hi), space: 32 (over y_lo, z, core).
Axes of the slice: x: 4, y: 4 (y_hi: 2, y_lo: 2; y = y_hi * 2 + y_lo), z: 8, core: 2. Of those that a mesh axis runs over, the one named last changes fastest.
Arguments:
- ensemble: bfloat16 [256, 48, 16384], P('member', None, 'space')
- inflation: float32 [256, 128], P('member'), may hold values from 0.5 to 2
- weights: bfloat16 [128, 256, 256], P('space')
- region_ids: int32 [16384], P('space'), may hold values from 0 to 127, as said below
- extinction: float32 [48], replicated, may hold values from 0.1 to 2
- obs_cols: int32 [4096], P('space'), may hold values from 0 to 16383, as said below
Outputs:
- analysis: bfloat16 [256, 48, 16384], P('member', None, 'space')
- obs_analysis: float32 [256, 4096], P('member', 'space')
Inputs may be any that keep to these rules, and one draw needn't show every extreme that they name: `region_ids`: region r belongs to index r // 4 of space. Each block of 512 columns held by one index of space holds exactly 16 columns of the regions of every index of space. `obs_cols`: each observation's column lies in the block of 512 columns held by the same index of space as the observation.
All inputs are finite; a program needn't handle non-finite values.
Results may differ from a plain program's by a relative error of at most 0.0047.
Values may be sent and summed in bfloat16 or wider, within the bound.
No kernel may reach another device: no remote copies, remote signals or barrier semaphores. Data moves between devices by JAX's collectives and lax.ppermute only.
A program may use at most 64 MiB of HBM per device.

v0:
```python
import jax
import jax.numpy as jnp
from jax import lax
from jax.sharding import PartitionSpec as P


def _split3(x):
    hi = lax.reduce_precision(x, exponent_bits=8, mantissa_bits=7)
    r1 = x - hi
    mid = lax.reduce_precision(r1, exponent_bits=8, mantissa_bits=7)
    lo = r1 - mid
    return (hi.astype(jnp.bfloat16), mid.astype(jnp.bfloat16), lo.astype(jnp.bfloat16))


def local(ensemble, inflation, weights, region_ids, extinction, obs_cols):
    n_space = lax.axis_size("space")
    n_member = lax.axis_size("member")
    local_members = ensemble.shape[0]
    tracers = ensemble.shape[1]
    columns = ensemble.shape[2]
    members = local_members * n_member
    reg_count = weights.shape[0]
    all_regions = inflation.shape[1]
    send_cols = columns // n_space
    slot_cols = send_cols // n_member
    own_cols = n_space * slot_cols
    row_len = local_members * tracers
    extra_len = 128
    owner = region_ids // reg_count
    owner_hot = (owner[:, None] == jnp.arange(n_space, dtype=jnp.int32)[None, :]).astype(jnp.int32)
    before = jnp.cumsum(owner_hot, axis=0) - owner_hot
    rank_in = jnp.sum(before * owner_hot, axis=1)
    position = owner * send_cols + rank_in
    ordering = (
        jnp.zeros((columns,), jnp.int32).at[position].set(jnp.arange(columns, dtype=jnp.int32))
    )
    region_hot = (jnp.arange(all_regions, dtype=jnp.int32)[:, None] == region_ids[None, :]).astype(
        jnp.float32
    )
    factor = jnp.dot(inflation, region_hot, precision=lax.Precision.HIGHEST)
    f_hi, f_mid, f_lo = _split3(factor.T)
    label = (region_ids % reg_count).astype(jnp.bfloat16)[:, None]
    pad = jnp.zeros((columns, extra_len - 3 * local_members - 1), jnp.bfloat16)
    extra = jnp.concatenate([f_hi, f_mid, f_lo, label, pad], axis=1)
    rows_major = jnp.transpose(ensemble, (2, 0, 1)).reshape(columns, row_len)
    rows = jnp.concatenate([rows_major, extra], axis=1)
    width = row_len + extra_len
    payload = jnp.take(rows, ordering, axis=0).reshape(n_space, n_member, slot_cols, width)
    received = lax.all_to_all(
        lax.all_to_all(payload, "member", split_axis=1, concat_axis=3, tiled=True),
        "space",
        split_axis=0,
        concat_axis=0,
        tiled=True,
    )
    gathered = received.reshape(own_cols, n_member, width)
    ens_part = gathered[:, :, :row_len].reshape(own_cols, members, tracers)
    ext = gathered[:, :, row_len:].astype(jnp.float32)
    lm = local_members
    fac = (ext[:, :, 0:lm] + ext[:, :, lm : 2 * lm] + ext[:, :, 2 * lm : 3 * lm]).reshape(
        own_cols, members
    )
    got_labels = ext[:, 0, 3 * lm].astype(jnp.int32)
    ens32 = ens_part.astype(jnp.float32)
    mean = jnp.sum(ens32, axis=1) / members
    anomaly = ((ens32 - mean[:, None, :]) * fac[:, :, None]).astype(jnp.bfloat16)
    accum = jnp.zeros((own_cols, members, tracers), jnp.float32)
    for region in range(reg_count):
        partial_prod = jnp.einsum(
            "jk,cjt->ckt", weights[region], anomaly, preferred_element_type=jnp.float32
        )
        accum = accum + jnp.where((got_labels == region)[:, None, None], partial_prod, 0.0)
    increment = accum.astype(jnp.bfloat16)
    result_rows = (mean[:, None, :] + increment.astype(jnp.float32)).astype(jnp.bfloat16)
    result_rows = result_rows.reshape(n_space, 1, slot_cols, members * tracers)
    halfway = lax.all_to_all(result_rows, "space", split_axis=0, concat_axis=0, tiled=True)
    returned = lax.all_to_all(halfway, "member", split_axis=3, concat_axis=1, tiled=True)
    restored = jnp.take(returned.reshape(columns, local_members * tracers), position, axis=0)
    analysis = jnp.transpose(restored.reshape(columns, local_members, tracers), (1, 2, 0))
    local_index = obs_cols - lax.axis_index("space") * columns
    picked = jnp.take(analysis, local_index, axis=2).astype(jnp.float32)
    obs_analysis = jnp.einsum("t,kto->ko", extinction, picked, precision=lax.Precision.HIGHEST)
    return (analysis, obs_analysis)


def solution(mesh):
    in_specs = (
        P("member", None, "space"),
        P("member", None),
        P("space", None, None),
        P("space"),
        P(),
        P("space"),
    )
    out_specs = (P("member", None, "space"), P("member", "space"))
    return jax.shard_map(local, mesh=mesh, in_specs=in_specs, out_specs=out_specs, check_vma=False)
```

profile of v0, /device:TPU:64, one launch (start us, length us, event | category | flops | bytes accessed | tf_op | source)
XLA Modules:
  0.0 318.0 jit_solution(428694375917716117)
XLA Ops:
  3.5 2.4 scatter_custom_fusion
  12.6 2.1 concatenate.3
  14.7 2.3 gather_fusion
  18.2 30.9 %all_to_all.43 = bf16[32,8,2,1664]{3,0,2,1:T(8,128)(2,1)S(1)} all-to-all(bf16[32,8,2,1664]{3,0,2,1:T(8,128)(2,1)S(1)} %copy_select_fusion), channel_id=1, replica_groups=mesh['member'=8,'space'=32] {'member'}, dimensions={1} | all-to-all | bytes 3407872 | tf_op jit(solution)/shard_map/all_to_all | solution.py:50
  50.5 49.5 %all_to_all.44 = bf16[32,1,2,13312]{3,2,1,0:T(2,128)(2,1)} all-to-all(bf16[32,1,2,13312]{3,2,1,0:T(2,128)(2,1)S(1)} %reshape.130), channel_id=1, replica_groups=mesh['member'=8,'space'=32] {'space'}, dimensions={0} | all-to-all | bytes 3407872 | tf_op jit(solution)/shard_map/all_to_all | solution.py:49
  100.0 4.2 %reshape.84 = bf16[64,8,1664]{2,1,0:T(8,128)(2,1)S(1)} reshape(bf16[32,1,2,13312]{3,2,1,0:T(2,128)(2,1)} %all_to_all.44) | data formatting | bytes 3407872 | tf_op jit(solution)/shard_map/reshape | solution.py:56
  104.2 4.7 %compare_reduce_fusion.3 = (pred[64]{0:T(512)(128)(4,1)S(1)}, pred[64]{0:T(512)(128)(4,1)S(1)}, pred[64]{0:T(512)(128)(4,1)S(1)}, pred[64]{0:T(512)(128)(4,1)S(1)}) fusion(f32[64,8,128]{2,1,0:T(8,128)S(1)} %slice_convert_fusion.1), kind=kLoop, calls=%fused_computation.34 | loop fusion | flops 320 | bytes 512 | tf_op jit(solution)/shard_map/eq | solution.py:72
  109.2 2.2 slice_convert_fusion
  111.6 7.5 %reshape.87 = f32[64,256,48]{2,1,0:T(8,128)} reshape(f32[64,8,1536]{2,1,0:T(8,128)} %slice_convert_fusion) | data formatting | bytes 6291456 | tf_op jit(solution)/shard_map/convert_element_type | solution.py:64
  119.1 4.5 %reduce_sum.19 = f32[64,48]{1,0:T(8,128)S(1)} reduce(f32[64,256,48]{2,1,0:T(8,128)} %reshape.87, f32[]{:T(128)} %constant.89.clone.1), dimensions={1}, to_apply=%region_4.5 | reduce | flops 783360 | bytes 3158020 | tf_op jit(solution)/shard_map/reduce_sum | solution.py:65
  123.6 4.6 %mul.32 = f32[64,256,48]{2,1,0:T(8,128)} broadcast(f32[64,256]{1,0:T(8,128)S(1)} %copy.90), dimensions={0,1} | broadcast | bytes 3211264 | tf_op jit(solution)/shard_map/mul | solution.py:66
  128.2 9.0 %mul.33 = f32[64,8,1536]{2,1,0:T(8,128)} reshape(f32[64,256,48]{2,1,0:T(8,128)} %mul.32) | data formatting | bytes 6291456 | tf_op jit(solution)/shard_map/mul | solution.py:66
  137.2 3.8 %add.69 = f32[64,256,48]{2,1,0:T(8,128)} broadcast(f32[64,48]{1,0:T(8,128)S(1)} %broadcast_multiply_fusion), dimensions={0,2} | broadcast | bytes 3158016 | tf_op jit(solution)/shard_map/add | solution.py:74
  141.0 9.1 %add.70 = f32[64,8,1536]{2,1,0:T(8,128)} reshape(f32[64,256,48]{2,1,0:T(8,128)} %add.69) | data formatting | bytes 6291456 | tf_op jit(solution)/shard_map/add | solution.py:74
  150.1 3.6 %multiply_convert_fusion = bf16[64,8,1536]{2,1,0:T(8,128)(2,1)S(1)} fusion(f32[64,8,1536]{2,1,0:T(8,128)} %mul.33, f32[64,8,1536]{2,1,0:T(8,128)} %add.70, bf16[64,8,1664]{2,1,0:T(8,128)(2,1)S(1)} %reshape.84), kind=kLoop, calls=%fused_computation.7 | loop fusion | flops 3145728 | bytes 9437184 | tf_op jit(solution)/shard_map/convert_element_type | solution.py:66
  153.7 5.5 %convert_element_type.71 = bf16[64,256,48]{2,1,0:T(8,128)(2,1)} reshape(bf16[64,8,1536]{2,1,0:T(8,128)(2,1)S(1)} %multiply_convert_fusion) | data formatting | bytes 3145728 | tf_op jit(solution)/shard_map/convert_element_type | solution.py:66
  159.2 3.6 %fusion.5 = f32[64,48,256]{2,1,0:T(8,128)S(1)} fusion(bf16[64,256,48]{2,1,0:T(8,128)(2,1)} %convert_element_type.71, bf16[4,256,256]{2,1,0:T(8,128)(2,1)S(1)} %copy-done.3), kind=kOutput, calls=%fused_computation.20 | convolution fusion | flops 402653184 | bytes 4849664 | tf_op jit(solution)/shard_map/jk,cjt->ckt/dot_general | solution.py:69
  165.4 3.2 %fusion = bf16[64,256,48]{1,2,0:T(8,128)(2,1)S(1)} fusion(f32[64,48]{1,0:T(8,128)S(1)} %broadcast_multiply_fusion, bf16[64,256,48]{2,1,0:T(8,128)(2,1)S(1)} %copy-done.2, pred[64]{0:T(512)(128)(4,1)S(1)} %get-tuple-element.13, f32[64,48,256]{2,1,0:T(8,128)S(1)} %fusion.5, pred[64]{0:T(512)(128)(4,1)S(1)} %get-tuple-element.12, ...), kind=kOutput, calls=%fused_computation.9 | convolution fusion | flops 411303936 | bytes 12726528 | tf_op jit(solution)/shard_map/jk,cjt->ckt/dot_general | solution.py:69
  168.6 3.2 copy.95
  171.7 9.3 %reshape.85 = bf16[32,1,2,12288]{3,2,0,1:T(2,128)(2,1)S(1)} reshape(bf16[64,256,48]{2,1,0:T(8,128)(2,1)} %copy.95) | data formatting | bytes 3145728 | tf_op jit(solution)/shard_map/reshape | solution.py:75
  181.0 43.6 %all_to_all.45 = bf16[32,1,2,12288]{3,2,1,0:T(2,128)(2,1)S(1)} all-to-all(bf16[32,1,2,12288]{3,2,1,0:T(2,128)(2,1)S(1)} %bitcast.75), channel_id=1, replica_groups=mesh['member'=8,'space'=32] {'space'}, dimensions={0} | all-to-all | bytes 3145728 | tf_op jit(solution)/shard_map/all_to_all | solution.py:76
  224.6 11.1 %copy.97 = bf16[32,1,2,12288]{0,2,1,3:T(2,128)(2,1)} copy(bf16[32,1,2,12288]{3,2,1,0:T(2,128)(2,1)S(1)} %all_to_all.45) | data formatting | bytes 3145728 | tf_op jit(solution)/shard_map/all_to_all | solution.py:76
  235.7 9.5 %reshape.138 = bf16[8,2,49152]{2,1,0:T(2,128)(2,1)} reshape(bf16[12288,1,2,32]{3,2,1,0:T(2,128)(2,1)} %bitcast.72) | data formatting | bytes 3145728
  245.2 4.0 %all-to-all-start.3 = ((bf16[8,2,49152]{2,1,0:T(2,128)(2,1)}), bf16[8,2,49152]{2,1,0:T(2,128)(2,1)S(1)}, u32[]{:S(2)}, u32[]{:S(2)}) async-start(bf16[8,2,49152]{2,1,0:T(2,128)(2,1)} %reshape.138), calls=%async_computation.3 | async-start | bytes 3145728 | tf_op jit(solution)/shard_map/all_to_all | solution.py:77
  249.3 24.1 %all-to-all-done.3 = bf16[8,2,49152]{2,1,0:T(2,128)(2,1)S(1)} async-done(((bf16[8,2,49152]{2,1,0:T(2,128)(2,1)}), bf16[8,2,49152]{2,1,0:T(2,128)(2,1)S(1)}, u32[]{:S(2)}, u32[]{:S(2)}) %all-to-all-start.3) | async-done | bytes 1572896 | tf_op jit(solution)/shard_map/all_to_all | solution.py:77
  273.4 5.4 %reshape.139 = bf16[12288,1,2,32]{3,2,1,0:T(2,128)(2,1)} reshape(bf16[8,2,49152]{2,1,0:T(2,128)(2,1)S(1)} %all-to-all-done.3) | data formatting | bytes 3145728
  278.8 14.4 %copy.98 = bf16[32,1,2,8,1536]{4,2,3,0,1:T(2,128)(2,1)S(1)} copy(bf16[32,1,2,8,1536]{0,2,4,3,1:T(2,128)(2,1)} %bitcast.73) | data formatting | bytes 3145728 | tf_op jit(solution)/shard_map/all_to_all | solution.py:77
  293.9 2.1 gather_fusion.1
  296.8 6.5 %copy.100 = bf16[512,32,48]{2,1,0:T(8,128)(2,1)} copy(bf16[512,32,48]{0,2,1:T(8,128)(2,1)S(1)} %bitcast.76) | data formatting | bytes 3145728 | tf_op jit(solution)/shard_map/jit(_take)/gather | solution.py:78
  303.3 4.5 %select_bitcast_fusion = bf16[32,48,512]{1,0,2:T(8,128)(2,1)} fusion(bf16[512,32,48]{2,1,0:T(8,128)(2,1)} %copy.100, pred[512]{0:T(512)(128)(4,1)S(1)} %copy-done.8), kind=kLoop, calls=%fused_computation.4 | loop fusion | flops 786432 | bytes 3146240 | tf_op jit(solution)/shard_map/transpose | solution.py:79
  307.8 5.4 %copy.101 = bf16[32,48,512]{2,1,0:T(8,128)(2,1)} copy(bf16[32,48,512]{1,0,2:T(8,128)(2,1)} %select_bitcast_fusion) | data formatting | bytes 3145728
  313.2 2.9 gather_fusion.2
  (61 shorter events, 18.2 us)
Async XLA Ops:
  0.6 6.9 %copy-start = (f32[32,128]{1,0:T(8,128)S(1)}, f32[32,128]{1,0:T(8,128)}, u32[]{:S(2)}) copy-start(f32[32,128]{1,0:T(8,128)} %param.7) | copy-start | bytes 49156
  3.5 2.5 copy-start.6
  10.2 4.5 %copy-start.5 = (s32[1024]{0:T(1024)S(1)}, s32[1024]{0:T(1024)}, u32[]{:S(2)}) copy-start(s32[1024]{0:T(1024)} %pad_clamp_fusion.2) | copy-start | bytes 12292
  17.0 0.7 copy-start.4
  153.7 5.5 %copy-start.3 = (bf16[4,256,256]{2,1,0:T(8,128)(2,1)S(1)}, bf16[4,256,256]{2,1,0:T(8,128)(2,1)}, u32[]{:S(2)}) copy-start(bf16[4,256,256]{2,1,0:T(8,128)(2,1)} %param.8) | copy-start | bytes 1572868
  159.2 3.6 %copy-start.2 = (bf16[64,256,48]{2,1,0:T(8,128)(2,1)S(1)}, bf16[64,256,48]{2,1,0:T(8,128)(2,1)}, u32[]{:S(2)}) copy-start(bf16[64,256,48]{2,1,0:T(8,128)(2,1)} %convert_element_type.71) | copy-start | bytes 4718596
  245.2 4.0 %copy-start.7 = (s32[512]{0:T(512)S(1)}, s32[512]{0:T(512)}, u32[]{:S(2)}) copy-start(s32[512]{0:T(512)} %copy-done.6) | copy-start | bytes 6148
  245.2 4.0 %copy-start.10 = (s32[128]{0:T(128)S(1)}, s32[128]{0:T(128)}, u32[]{:S(2)}) copy-start(s32[128]{0:T(128)} %param.11) | copy-start | bytes 1540
  245.2 28.2 %all-to-all-start.3 = ((bf16[8,2,49152]{2,1,0:T(2,128)(2,1)}), bf16[8,2,49152]{2,1,0:T(2,128)(2,1)S(1)}, u32[]{:S(2)}, u32[]{:S(2)}) async-start(bf16[8,2,49152]{2,1,0:T(2,128)(2,1)} %reshape.138), calls=%async_computation.3 | async-start | bytes 3145728 | tf_op jit(solution)/shard_map/all_to_all | solution.py:77
  296.8 6.5 %copy-start.8 = (pred[512]{0:T(512)(128)(4,1)S(1)}, pred[512]{0:T(512)(128)(4,1)}, u32[]{:S(2)}) copy-start(pred[512]{0:T(512)(128)(4,1)} %get-tuple-element.16) | copy-start | bytes 1540
  307.8 8.5 %copy-start.9 = (f32[48]{0:T(128)S(1)}, f32[48]{0:T(128)}, u32[]{:S(2)}) copy-start(f32[48]{0:T(128)} %param.10) | copy-start | bytes 580
  307.8 10.1 %copy-start.1 = (f32[32,128]{1,0:T(8,128)S(1)}, f32[32,128]{1,0:T(8,128)}, u32[]{:S(2)}) copy-start(f32[32,128]{1,0:T(8,128)} %param.7) | copy-start | bytes 49156
where the time goes:
time: 320 us; the launch traced here: 318 us
  local copies, waits for them, and re-layouts  129 us (40%)
  blocking collectives  124 us (39%)
  waiting for transfers between devices  24.1 us (8%)
  other arithmetic  23.7 us (7%)
  matrix products  11.8 us (4%)
  starting transfers between devices  3.97 us (1%)
    all_to_all x1, blocking collectives, local(): lax.all_to_all(lax.all_to_all(payload, 'member', split_axis=1, concat_axi...  49.5 us
    all_to_all x1, blocking collectives, local(): lax.all_to_all(result_rows, 'space', split_axis=0, concat_axis=0, tiled=T...  43.6 us
    all_to_all x1, blocking collectives, local(): lax.all_to_all(payload, 'member', split_axis=1, concat_axis=3, tiled=True)  30.9 us
    all_to_all x1, waiting for transfers between devices, local(): lax.all_to_all(halfway, 'member', split_axis=3, concat_axis=1, tiled=True)  24.1 us
    unnamed x25, local copies, waits for them, and re-layouts  20.4 us
    all_to_all x1, local copies, waits for them, and re-layouts, local(): lax.all_to_all(halfway, 'member', split_axis=3, concat_axis=1, tiled=True)  14.4 us
    mul x3, local copies, waits for them, and re-layouts, local(): (ens32 - mean[:, None, :]) * fac[:, :, None]  13.7 us
    add x2, local copies, waits for them, and re-layouts, local(): mean[:, None, :] + increment.astype(jnp.float32)  12.8 us
  transfers between devices with their start and end apart: 1, of which 1 were waited for; matrix products, arithmetic and copies ran while one was open for 0% of the time, Pallas kernels for 0%

commit v1 on v0

--- a/solution.py
+++ b/solution.py
@@ -74,7 +74,10 @@
     result_rows = (mean[:, None, :] + increment.astype(jnp.float32)).astype(jnp.bfloat16)
     result_rows = result_rows.reshape(n_space, 1, slot_cols, members * tracers)
     halfway = lax.all_to_all(result_rows, "space", split_axis=0, concat_axis=0, tiled=True)
-    returned = lax.all_to_all(halfway, "member", split_axis=3, concat_axis=1, tiled=True)
+    size = lax.axis_size("member")
+    blocks = jnp.stack(jnp.split(halfway, size, axis=3), axis=0)
+    blocks = lax.all_to_all(blocks, "member", split_axis=0, concat_axis=0)
+    returned = jnp.concatenate(blocks, axis=1)
     restored = jnp.take(returned.reshape(columns, local_members * tracers), position, axis=0)
     analysis = jnp.transpose(restored.reshape(columns, local_members, tracers), (1, 2, 0))
     local_index = obs_cols - lax.axis_index("space") * columns

time: 320 us -> 287 us (0.90)
  local copies, waits for them, and re-layouts: 129 us -> 97 us
    all_to_all x2 -> x0, local copies, waits for them, and re-layouts: 25.5 us -> none  [the longest x1 14.4 us: local(): lax.all_to_all(halfway, 'member', split_axis=3, concat_axis=1, tiled=True)]
    unnamed x25 -> x30, local copies, waits for them, and re-layouts: 20.4 us -> 11.1 us
where the time goes in v1:
time: 287 us; the launch traced here: 286 us
  blocking collectives  124 us (43%)
  local copies, waits for them, and re-layouts  97 us (34%)
  waiting for transfers between devices  24.1 us (8%)
  other arithmetic  23.7 us (8%)
  matrix products  11.8 us (4%)
  starting transfers between devices  3.84 us (1%)
    all_to_all x1, blocking collectives, local(): lax.all_to_all(lax.all_to_all(payload, 'member', split_axis=1, concat_axi...  49.5 us
    all_to_all x1, blocking collectives, local(): lax.all_to_all(result_rows, 'space', split_axis=0, concat_axis=0, tiled=T...  43.6 us
    all_to_all x1, blocking collectives, local(): lax.all_to_all(payload, 'member', split_axis=1, concat_axis=3, tiled=True)  30.9 us
    all_to_all x1, waiting for transfers between devices, local(): blocks = lax.all_to_all(blocks, 'member', split_axis=0, concat_axis=0)  24.1 us
    mul x3, local copies, waits for them, and re-layouts, local(): (ens32 - mean[:, None, :]) * fac[:, :, None]  13.7 us
    add x2, local copies, waits for them, and re-layouts, local(): mean[:, None, :] + increment.astype(jnp.float32)  12.8 us
    unnamed x30, local copies, waits for them, and re-layouts  11.1 us
    gather x3, local copies, waits for them, and re-layouts, local(): jnp.take(returned.reshape(columns, local_members * tracers), position, ax...  9.38 us
  transfers between devices with their start and end apart: 1, of which 1 were waited for; matrix products, arithmetic and copies ran while one was open for 0% of the time, Pallas kernels for 0%

profile of v1, /device:TPU:64, one launch (start us, length us, event | category | flops | bytes accessed | tf_op | source)
XLA Modules:
  0.0 285.5 jit_solution(3586308878990334304)
XLA Ops:
  3.5 2.4 scatter_custom_fusion
  10.2 1.7 copy.65
  12.6 2.1 concatenate.3
  14.7 2.3 gather_fusion
  18.2 30.9 %all_to_all.33 = bf16[32,8,2,1664]{3,0,2,1:T(8,128)(2,1)S(1)} all-to-all(bf16[32,8,2,1664]{3,0,2,1:T(8,128)(2,1)S(1)} %copy_select_fusion), channel_id=1, replica_groups=mesh['member'=8,'space'=32] {'member'}, dimensions={1} | all-to-all | bytes 3407872 | tf_op jit(solution)/shard_map/all_to_all | solution.py:50
  50.5 49.5 %all_to_all.34 = bf16[32,1,2,13312]{3,2,1,0:T(2,128)(2,1)} all-to-all(bf16[32,1,2,13312]{3,2,1,0:T(2,128)(2,1)S(1)} %reshape.129), channel_id=1, replica_groups=mesh['member'=8,'space'=32] {'space'}, dimensions={0} | all-to-all | bytes 3407872 | tf_op jit(solution)/shard_map/all_to_all | solution.py:49
  100.0 4.2 %reshape.83 = bf16[64,8,1664]{2,1,0:T(8,128)(2,1)S(1)} reshape(bf16[32,1,2,13312]{3,2,1,0:T(2,128)(2,1)} %all_to_all.34) | data formatting | bytes 3407872 | tf_op jit(solution)/shard_map/reshape | solution.py:56
  104.2 4.7 %compare_reduce_fusion.3 = (pred[64]{0:T(512)(128)(4,1)S(1)}, pred[64]{0:T(512)(128)(4,1)S(1)}, pred[64]{0:T(512)(128)(4,1)S(1)}, pred[64]{0:T(512)(128)(4,1)S(1)}) fusion(f32[64,8,128]{2,1,0:T(8,128)S(1)} %slice_convert_fusion.1), kind=kLoop, calls=%fused_computation.50 | loop fusion | flops 320 | bytes 512 | tf_op jit(solution)/shard_map/eq | solution.py:72
  109.2 2.2 slice_convert_fusion
  111.6 7.5 %reshape.86 = f32[64,256,48]{2,1,0:T(8,128)} reshape(f32[64,8,1536]{2,1,0:T(8,128)} %slice_convert_fusion) | data formatting | bytes 6291456 | tf_op jit(solution)/shard_map/convert_element_type | solution.py:64
  119.1 4.5 %reduce_sum.19 = f32[64,48]{1,0:T(8,128)S(1)} reduce(f32[64,256,48]{2,1,0:T(8,128)} %reshape.86, f32[]{:T(128)} %constant.89.clone.1), dimensions={1}, to_apply=%region_4.5 | reduce | flops 783360 | bytes 3158020 | tf_op jit(solution)/shard_map/reduce_sum | solution.py:65
  123.6 4.6 %mul.32 = f32[64,256,48]{2,1,0:T(8,128)} broadcast(f32[64,256]{1,0:T(8,128)S(1)} %copy.74), dimensions={0,1} | broadcast | bytes 3211264 | tf_op jit(solution)/shard_map/mul | solution.py:66
  128.2 9.0 %mul.33 = f32[64,8,1536]{2,1,0:T(8,128)} reshape(f32[64,256,48]{2,1,0:T(8,128)} %mul.32) | data formatting | bytes 6291456 | tf_op jit(solution)/shard_map/mul | solution.py:66
  137.2 3.8 %add.69 = f32[64,256,48]{2,1,0:T(8,128)} broadcast(f32[64,48]{1,0:T(8,128)S(1)} %broadcast_multiply_fusion), dimensions={0,2} | broadcast | bytes 3158016 | tf_op jit(solution)/shard_map/add | solution.py:74
  141.0 9.1 %add.70 = f32[64,8,1536]{2,1,0:T(8,128)} reshape(f32[64,256,48]{2,1,0:T(8,128)} %add.69) | data formatting | bytes 6291456 | tf_op jit(solution)/shard_map/add | solution.py:74
  150.0 3.6 %multiply_convert_fusion = bf16[64,8,1536]{2,1,0:T(8,128)(2,1)S(1)} fusion(f32[64,8,1536]{2,1,0:T(8,128)} %mul.33, f32[64,8,1536]{2,1,0:T(8,128)} %add.70, bf16[64,8,1664]{2,1,0:T(8,128)(2,1)S(1)} %reshape.83), kind=kLoop, calls=%fused_computation.7 | loop fusion | flops 3145728 | bytes 9437184 | tf_op jit(solution)/shard_map/convert_element_type | solution.py:66
  153.7 5.5 %convert_element_type.71 = bf16[64,256,48]{2,1,0:T(8,128)(2,1)} reshape(bf16[64,8,1536]{2,1,0:T(8,128)(2,1)S(1)} %multiply_convert_fusion) | data formatting | bytes 3145728 | tf_op jit(solution)/shard_map/convert_element_type | solution.py:66
  159.2 3.6 %fusion.13 = f32[64,48,256]{2,1,0:T(8,128)S(1)} fusion(bf16[64,256,48]{2,1,0:T(8,128)(2,1)} %convert_element_type.71, bf16[4,256,256]{2,1,0:T(8,128)(2,1)S(1)} %copy-done.3), kind=kOutput, calls=%fused_computation.36 | convolution fusion | flops 402653184 | bytes 4849664 | tf_op jit(solution)/shard_map/jk,cjt->ckt/dot_general | solution.py:69
  164.1 1.3 fusion.17
  165.4 3.2 %fusion = bf16[64,256,48]{1,2,0:T(8,128)(2,1)S(1)} fusion(f32[64,48]{1,0:T(8,128)S(1)} %broadcast_multiply_fusion, bf16[64,256,48]{2,1,0:T(8,128)(2,1)S(1)} %copy-done.2, pred[64]{0:T(512)(128)(4,1)S(1)} %get-tuple-element.11, f32[64,48,256]{2,1,0:T(8,128)S(1)} %fusion.13, pred[64]{0:T(512)(128)(4,1)S(1)} %get-tuple-element.10, ...), kind=kOutput, calls=%fused_computation.9 | convolution fusion | flops 411303936 | bytes 12726528 | tf_op jit(solution)/shard_map/jk,cjt->ckt/dot_general | solution.py:69
  168.6 3.2 %copy.79 = bf16[64,256,48]{2,1,0:T(8,128)(2,1)} copy(bf16[64,256,48]{1,2,0:T(8,128)(2,1)S(1)} %fusion) | data formatting | bytes 3145728 | tf_op jit(solution)/shard_map/convert_element_type | solution.py:74
  171.7 9.3 %reshape.84 = bf16[32,1,2,12288]{3,2,0,1:T(2,128)(2,1)S(1)} reshape(bf16[64,256,48]{2,1,0:T(8,128)(2,1)} %copy.79) | data formatting | bytes 3145728 | tf_op jit(solution)/shard_map/reshape | solution.py:75
  181.0 43.6 %all_to_all.35 = bf16[32,1,2,12288]{3,2,1,0:T(2,128)(2,1)S(1)} all-to-all(bf16[32,1,2,12288]{3,2,1,0:T(2,128)(2,1)S(1)} %bitcast.117), channel_id=1, replica_groups=mesh['member'=8,'space'=32] {'space'}, dimensions={0} | all-to-all | bytes 3145728 | tf_op jit(solution)/shard_map/all_to_all | solution.py:76
  231.1 3.8 %all-to-all-start.3 = ((bf16[8,32,1,2,1536]{4,3,1,2,0:T(2,128)(2,1)}), bf16[8,32,1,2,1536]{4,3,1,2,0:T(2,128)(2,1)S(1)}, u32[]{:S(2)}, u32[]{:S(2)}) async-start(bf16[8,32,1,2,1536]{4,3,1,2,0:T(2,128)(2,1)} %fusion.4), calls=%async_computation.3 | async-start | bytes 3145728 | tf_op jit(solution)/shard_map/all_to_all | solution.py:79
  235.1 24.1 %all-to-all-done.3 = bf16[8,32,1,2,1536]{4,3,1,2,0:T(2,128)(2,1)S(1)} async-done(((bf16[8,32,1,2,1536]{4,3,1,2,0:T(2,128)(2,1)}), bf16[8,32,1,2,1536]{4,3,1,2,0:T(2,128)(2,1)S(1)}, u32[]{:S(2)}, u32[]{:S(2)}) %all-to-all-start.3) | async-done | bytes 1572896 | tf_op jit(solution)/shard_map/all_to_all | solution.py:79
  259.2 1.6 copy.88
  261.4 2.1 gather_fusion.1
  264.3 6.5 %copy.90 = bf16[512,32,48]{2,1,0:T(8,128)(2,1)} copy(bf16[512,32,48]{0,2,1:T(8,128)(2,1)S(1)} %bitcast.118) | data formatting | bytes 3145728 | tf_op jit(solution)/shard_map/jit(_take)/gather | solution.py:81
  270.9 4.5 %select_bitcast_fusion = bf16[32,48,512]{1,0,2:T(8,128)(2,1)} fusion(bf16[512,32,48]{2,1,0:T(8,128)(2,1)} %copy.90, pred[512]{0:T(512)(128)(4,1)S(1)} %copy-done.8), kind=kLoop, calls=%fused_computation.4 | loop fusion | flops 786432 | bytes 3146240 | tf_op jit(solution)/shard_map/transpose | solution.py:82
  275.4 5.3 %copy.91 = bf16[32,48,512]{2,1,0:T(8,128)(2,1)} copy(bf16[32,48,512]{1,0,2:T(8,128)(2,1)} %select_bitcast_fusion) | data formatting | bytes 3145728
  280.7 3.0 %gather_fusion.2 = bf16[128,32,48]{2,1,0:T(8,128)(2,1)S(1)} fusion(bf16[32,48,512]{1,0,2:T(8,128)(2,1)} %select_bitcast_fusion, s32[1024]{0:T(1024)S(1)} %get-tuple-element.21), kind=kCustom, calls=%fused_computation.2 | custom fusion | bytes 786944 | tf_op jit(solution)/shard_map/jit(_take)/gather | solution.py:84
  283.9 1.6 fusion.1
  (65 shorter events, 20.1 us)
Async XLA Ops:
  0.6 6.9 %copy-start = (f32[32,128]{1,0:T(8,128)S(1)}, f32[32,128]{1,0:T(8,128)}, u32[]{:S(2)}) copy-start(f32[32,128]{1,0:T(8,128)} %param.7) | copy-start | bytes 49156
  3.5 2.5 copy-start.6
  12.6 2.1 copy-start.5
  17.0 0.7 copy-start.4
  153.7 5.5 %copy-start.3 = (bf16[4,256,256]{2,1,0:T(8,128)(2,1)S(1)}, bf16[4,256,256]{2,1,0:T(8,128)(2,1)}, u32[]{:S(2)}) copy-start(bf16[4,256,256]{2,1,0:T(8,128)(2,1)} %param.8) | copy-start | bytes 1572868
  159.2 3.6 %copy-start.2 = (bf16[64,256,48]{2,1,0:T(8,128)(2,1)S(1)}, bf16[64,256,48]{2,1,0:T(8,128)(2,1)}, u32[]{:S(2)}) copy-start(bf16[64,256,48]{2,1,0:T(8,128)(2,1)} %convert_element_type.71) | copy-start | bytes 4718596
  230.3 4.7 %copy-start.10 = (s32[128]{0:T(128)S(1)}, s32[128]{0:T(128)}, u32[]{:S(2)}) copy-start(s32[128]{0:T(128)} %param.11) | copy-start | bytes 1540
  230.3 4.7 %copy-start.7 = (s32[512]{0:T(512)S(1)}, s32[512]{0:T(512)}, u32[]{:S(2)}) copy-start(s32[512]{0:T(512)} %copy-done.6) | copy-start | bytes 6148
  231.1 28.0 %all-to-all-start.3 = ((bf16[8,32,1,2,1536]{4,3,1,2,0:T(2,128)(2,1)}), bf16[8,32,1,2,1536]{4,3,1,2,0:T(2,128)(2,1)S(1)}, u32[]{:S(2)}, u32[]{:S(2)}) async-start(bf16[8,32,1,2,1536]{4,3,1,2,0:T(2,128)(2,1)} %fusion.4), calls=%async_computation.3 | async-start | bytes 3145728 | tf_op jit(solution)/shard_map/all_to_all | solution.py:79
  264.3 6.5 %copy-start.8 = (pred[512]{0:T(512)(128)(4,1)S(1)}, pred[512]{0:T(512)(128)(4,1)}, u32[]{:S(2)}) copy-start(pred[512]{0:T(512)(128)(4,1)} %get-tuple-element.14) | copy-start | bytes 1540
  280.7 3.2 %copy-start.9 = (f32[48]{0:T(128)S(1)}, f32[48]{0:T(128)}, u32[]{:S(2)}) copy-start(f32[48]{0:T(128)} %param.10) | copy-start | bytes 580
  280.7 4.8 %copy-start.1 = (f32[32,128]{1,0:T(8,128)S(1)}, f32[32,128]{1,0:T(8,128)}, u32[]{:S(2)}) copy-start(f32[32,128]{1,0:T(8,128)} %param.7) | copy-start | bytes 49156
